TPU v7x, 32 devices: a whole 2x2x4 slice. The times are simulated.
32 devices in a mesh: req: 8 (over z, y), tp: 4 (over x, core).
Axes of the slice: x: 2, y: 2, z: 4, core: 2. Of those that a mesh axis runs over, the one named last changes fastest.
Arguments:
- tokens_in: bfloat16 [24, 4, 2048], P('req'), may hold values from -6 to 6
- attn_norm: bfloat16 [2048], replicated, may hold values from 0.099609375 to 1.8984375
- qkv_weight: bfloat16 [2048, 3, 2048], P(None, None, 'tp'), may hold values from -0.125 to 0.125
- qkv_bias: bfloat16 [3, 2048], P(None, 'tp'), may hold values from -12 to 12
- out_weight: bfloat16 [2048, 2048], P('tp'), may hold values from -0.125 to 0.125
- cache_keys: bfloat16 [320, 128, 2048], P('req', None, 'tp'), may hold values from -12 to 12
- cache_values: bfloat16 [320, 128, 2048], P('req', None, 'tp'), may hold values from -6 to 6
- page_table: int32 [24, 37], replicated, may hold values from -1 to 319, as said below
- cache_lengths: int32 [24], replicated, may hold values from 1 to 4736, as said below
- mlp_norm: bfloat16 [2048], replicated, may hold values from 0.099609375 to 1.8984375
- routes: int32 [24, 4, 4], P('req'), may hold values from 0 to 7, all different within a row; in each aligned block of 12 rows (0 to 11, 12 to 23, ..., all dimensions but the last counted through in order) at most 6 rows name the same one
- route_gates: float32 [24, 4, 4], P('req'), may hold values from 0.05 to 0.5
- expert_w_gate: bfloat16 [8, 2048, 1408], P('req', None, 'tp'), may hold values from -0.125 to 0.125
- expert_w_up: bfloat16 [8, 2048, 1408], P('req', None, 'tp'), may hold values from -0.125 to 0.125
- expert_w_down: bfloat16 [8, 1408, 2048], P('req', 'tp'), may hold values from -0.15625 to 0.15625
- shared_w_gate: bfloat16 [2048, 5632], P('tp', 'req'), may hold values from -0.125 to 0.125
- shared_w_up: bfloat16 [2048, 5632], P('tp', 'req'), may hold values from -0.125 to 0.125
- shared_w_down: bfloat16 [5632, 2048], P('req', 'tp'), may hold values from -0.078125 to 0.078125
- shared_switch: bfloat16 [2048], replicated, may hold values from -0.125 to 0.125
Outputs:
- layer_out: bfloat16 [24, 4, 2048], P('req', None, 'tp')
Inputs may be any that keep to these rules, and one draw needn't show every extreme that they name: `page_table`: entry [r, j] is the pool page holding positions j*128 to (j+1)*128 - 1 of request r's cache, or -1. No pool page is named twice. 6 requests, drawn from the seed, have all 37 entries set, all outside the first 12 pages of every block of 40 pool pages; every other request r has exactly its first 4 entries set, all among pool pages (r // 3)*40 to (r // 3)*40 + 3*4 - 1. `cache_lengths`: A long request has 2368 to 4736 cached tokens, any other 1 to 512; both largest values occur in every draw. `routes`: the 4 experts of a token differ. Among the 12 tokens of each aligned block of rows (those of one index of req) no expert is named more than 6 times, and in some of those blocks one expert is named exactly 6 times.
All inputs are finite; a program needn't handle non-finite values.
Results may differ from a plain program's by a relative error of at most 0.006.
Values may be sent and summed in bfloat16 or wider, within the bound.
No kernel may reach another device: no remote copies, remote signals or barrier semaphores. Data moves between devices by JAX's collectives and lax.ppermute only.
A program may use at most 128 MiB of HBM per device.

v0:
```python
import math
import jax
import jax.numpy as jnp
from jax import lax
from jax.sharding import PartitionSpec as P

HD = 128
TOPK = 4
NEG = -1e30
EPS = 1e-06
THETA = 1000000.0
HIGHEST = lax.Precision.HIGHEST


def rms_norm(inputs, gain_vector):
    values = inputs.astype(jnp.float32)
    scaled = values * lax.rsqrt(jnp.mean(values * values, axis=-1, keepdims=True) + EPS)
    return (scaled * gain_vector.astype(jnp.float32)).astype(jnp.bfloat16)


def rotate(values, positions):
    half_dim = values.shape[-1] // 2
    exponents = jnp.arange(half_dim, dtype=jnp.float32) * (2.0 / values.shape[-1])
    frequency = jnp.power(THETA, -exponents)
    angles = positions.astype(jnp.float32)[..., None, None] * frequency
    cosines = jnp.cos(angles)
    sine_part = jnp.sin(angles)
    front_half = values[..., :half_dim]
    back_half = values[..., half_dim:]
    return jnp.concatenate(
        [
            front_half * cosines - back_half * sine_part,
            back_half * cosines + front_half * sine_part,
        ],
        axis=-1,
    )


def bcast_a2a(values, axis, count):
    spread = jnp.broadcast_to(values[None], (count,) + values.shape)
    return lax.all_to_all(spread, axis, 0, 0, tiled=True).reshape(
        (count * values.shape[0],) + values.shape[1:]
    )


def per_device(
    tokens_in,
    attn_norm,
    qkv_weight,
    qkv_bias,
    out_weight,
    cache_keys,
    cache_values,
    page_table,
    cache_lengths,
    mlp_norm,
    routes,
    route_gates,
    expert_w_gate,
    expert_w_up,
    expert_w_down,
    shared_w_gate,
    shared_w_up,
    shared_w_down,
    shared_switch,
):
    req_rows, step_count, model_width = tokens_in.shape
    head_width = qkv_weight.shape[2]
    local_heads = head_width // HD
    req_count = lax.axis_size("req")
    tp_count = lax.axis_size("tp")
    req_index = lax.axis_index("req")
    tp_index = lax.axis_index("tp")
    all_requests = page_table.shape[0]
    pool_here = cache_keys.shape[0]
    page_len = cache_keys.shape[1]
    score_scale = 1.0 / math.sqrt(HD)
    col_share = model_width // tp_count
    row_count = req_rows * step_count
    normed = rms_norm(tokens_in, attn_norm)
    projected = jnp.einsum(
        "rsd,dcf->rscf", normed, qkv_weight, preferred_element_type=jnp.float32
    ) + qkv_bias.astype(jnp.float32)
    own_lengths = lax.dynamic_slice_in_dim(cache_lengths, req_index * req_rows, req_rows)
    positions = own_lengths[:, None] + jnp.arange(step_count, dtype=jnp.int32)[None, :]
    head_shape = (req_rows, step_count, local_heads, HD)
    query_new = rotate(projected[:, :, 0].reshape(head_shape), positions).astype(jnp.bfloat16)
    key_new = rotate(projected[:, :, 1].reshape(head_shape), positions).astype(jnp.bfloat16)
    value_new = projected[:, :, 2].reshape(head_shape).astype(jnp.bfloat16)
    query_all = bcast_a2a(query_new, "req", req_count)
    slot_ids = req_index * pool_here + jnp.arange(pool_here, dtype=jnp.int32)
    matches = (page_table[:, :, None] == slot_ids[None, None, :]).astype(jnp.int32)
    request_ids = jnp.arange(all_requests, dtype=jnp.int32)
    page_ids = jnp.arange(page_table.shape[1], dtype=jnp.int32)
    owner = jnp.sum(matches * request_ids[:, None, None], axis=(0, 1))
    logical = jnp.sum(matches * page_ids[None, :, None], axis=(0, 1))
    present = jnp.sum(matches, axis=(0, 1)) > 0
    token_pos = logical[:, None] * page_len + jnp.arange(page_len, dtype=jnp.int32)[None, :]
    live = present[:, None] & (token_pos < cache_lengths[owner][:, None])
    page_queries = query_all[owner]
    page_keys = cache_keys.reshape(pool_here, page_len, local_heads, HD)
    page_values = cache_values.reshape(pool_here, page_len, local_heads, HD)
    scores = (
        jnp.einsum("pshd,pkhd->pshk", page_queries, page_keys, preferred_element_type=jnp.float32)
        * score_scale
    )
    page_mask = live[:, None, None, :]
    masked = jnp.where(page_mask, scores, NEG)
    page_max = jnp.max(masked, axis=-1)
    weights = jnp.where(page_mask, jnp.exp(masked - page_max[..., None]), 0.0)
    page_sum = jnp.sum(weights, axis=-1)
    page_out = jnp.einsum(
        "pshk,pkhd->pshd",
        weights.astype(jnp.bfloat16),
        page_values,
        preferred_element_type=jnp.float32,
    )
    belongs = (owner[None, :] == request_ids[:, None]) & present[None, :]
    owned = belongs[:, :, None, None]
    local_max = jnp.max(jnp.where(owned, page_max[None], NEG), axis=1)
    factors = jnp.where(owned, jnp.exp(page_max[None] - local_max[:, None]), 0.0)
    local_out = jnp.einsum("rpsh,pshd->rshd", factors, page_out, precision=HIGHEST)
    local_sum = jnp.einsum("rpsh,psh->rsh", factors, page_sum, precision=HIGHEST)
    stat_width = step_count * local_heads
    stat_row = jnp.concatenate(
        [
            local_max.reshape(all_requests, stat_width),
            local_sum.reshape(all_requests, stat_width),
            jnp.zeros((all_requests, HD - 2 * stat_width), jnp.float32),
        ],
        axis=1,
    )
    packed = jnp.concatenate(
        [local_out.reshape(all_requests, stat_width, HD), stat_row[:, None, :]], axis=1
    )
    gathered = lax.all_to_all(packed, "req", 0, 0, tiled=True).reshape(
        req_count, req_rows, stat_width + 1, HD
    )
    part_out = gathered[:, :, :stat_width, :]
    part_max = gathered[:, :, stat_width, :stat_width]
    part_sum = gathered[:, :, stat_width, stat_width : 2 * stat_width]
    cache_max = jnp.max(part_max, axis=0)
    rescale = jnp.exp(part_max - cache_max[None])
    cache_out = jnp.sum(part_out * rescale[..., None], axis=0).reshape(
        req_rows, step_count, local_heads, HD
    )
    cache_sum = jnp.sum(part_sum * rescale, axis=0).reshape(req_rows, step_count, local_heads)
    cache_max = cache_max.reshape(req_rows, step_count, local_heads)
    new_scores = (
        jnp.einsum("rshd,rthd->rsht", query_new, key_new, preferred_element_type=jnp.float32)
        * score_scale
    )
    causal = jnp.arange(step_count)[:, None] >= jnp.arange(step_count)[None, :]
    new_mask = causal[None, :, None, :]
    new_masked = jnp.where(new_mask, new_scores, NEG)
    new_max = jnp.max(new_masked, axis=-1)
    new_weights = jnp.where(new_mask, jnp.exp(new_masked - new_max[..., None]), 0.0)
    new_sum = jnp.sum(new_weights, axis=-1)
    new_out = jnp.einsum(
        "rsht,rthd->rshd",
        new_weights.astype(jnp.bfloat16),
        value_new,
        preferred_element_type=jnp.float32,
    )
    top_max = jnp.maximum(cache_max, new_max)
    cache_factor = jnp.exp(cache_max - top_max)
    new_factor = jnp.exp(new_max - top_max)
    attended = (cache_out * cache_factor[..., None] + new_out * new_factor[..., None]) / (
        cache_sum * cache_factor + new_sum * new_factor
    )[..., None]
    attended = attended.astype(jnp.bfloat16).reshape(row_count, head_width)
    attn_part = jnp.dot(attended, out_weight, preferred_element_type=jnp.float32)
    attn_full = jnp.sum(
        bcast_a2a(attn_part, "tp", tp_count).reshape(tp_count, row_count, model_width), axis=0
    )
    resid = tokens_in.reshape(row_count, model_width).astype(jnp.float32) + attn_full
    mixed = rms_norm(resid, mlp_norm)
    expert_count = req_count * expert_w_gate.shape[0]
    capacity = max(2, (row_count * TOPK + expert_count - 1) // expert_count)
    picks = routes.reshape(row_count * TOPK)
    gates_flat = route_gates.reshape(row_count * TOPK)
    expert_hot = (picks[:, None] == jnp.arange(expert_count, dtype=jnp.int32)[None, :]).astype(
        jnp.int32
    )
    slot_index = jnp.sum((jnp.cumsum(expert_hot, axis=0) - 1) * expert_hot, axis=1)
    destination = picks * capacity + slot_index
    dest_hot = (
        destination[:, None] == jnp.arange(expert_count * capacity, dtype=jnp.int32)[None, :]
    ).astype(jnp.float32)
    token_hot = (
        (jnp.arange(row_count * TOPK, dtype=jnp.int32) // TOPK)[:, None]
        == jnp.arange(row_count, dtype=jnp.int32)[None, :]
    ).astype(jnp.float32)
    placement = jnp.einsum("cx,ct->xt", dest_hot, token_hot, precision=HIGHEST).astype(jnp.bfloat16)
    outgoing = jnp.dot(placement, mixed, preferred_element_type=jnp.float32).astype(jnp.bfloat16)
    combine_map = jnp.einsum(
        "ct,cx->tx", token_hot, dest_hot * gates_flat[:, None], precision=HIGHEST
    )
    w_gate_here = expert_w_gate[0]
    w_up_here = expert_w_up[0]
    w_down_here = expert_w_down[0]
    mixed_cols = lax.dynamic_slice_in_dim(mixed, tp_index * col_share, col_share, 1)
    shared_send = jnp.broadcast_to(mixed_cols[None], (req_count, row_count, col_share))
    dispatch = jnp.concatenate(
        [
            outgoing.reshape(req_count, capacity * model_width),
            shared_send.reshape(req_count, row_count * col_share),
        ],
        axis=1,
    )
    received = lax.all_to_all(dispatch, "req", 0, 0, tiled=True)
    item_count = capacity
    flat_rows = received[:, : capacity * model_width].reshape(req_count * capacity, model_width)
    piece = received[:, capacity * model_width :].reshape(req_count * row_count, col_share)
    gate_pre = jnp.dot(flat_rows, w_gate_here, preferred_element_type=jnp.float32)
    up_pre = jnp.dot(flat_rows, w_up_here, preferred_element_type=jnp.float32)
    hidden = (jax.nn.silu(gate_pre) * up_pre).astype(jnp.bfloat16)
    partial_out = jnp.dot(hidden, w_down_here, preferred_element_type=jnp.float32)
    expert_rows = req_count * capacity
    partial_split = partial_out.reshape(expert_rows, tp_count, col_share).transpose(1, 0, 2)
    gate_part = jnp.dot(piece, shared_w_gate, preferred_element_type=jnp.float32)
    up_part = jnp.dot(piece, shared_w_up, preferred_element_type=jnp.float32)
    unit_count = shared_w_gate.shape[1]
    all_rows = req_count * row_count
    expert_high = partial_split.astype(jnp.bfloat16)
    expert_low = (partial_split - expert_high.astype(jnp.float32)).astype(jnp.bfloat16)
    shared_pre = jnp.concatenate([gate_part, up_part], axis=1).astype(jnp.bfloat16)
    reduce_in = jnp.concatenate(
        [
            expert_high.reshape(tp_count, expert_rows * col_share),
            expert_low.reshape(tp_count, expert_rows * col_share),
            jnp.broadcast_to(
                shared_pre.reshape(1, all_rows * 2 * unit_count),
                (tp_count, all_rows * 2 * unit_count),
            ),
        ],
        axis=1,
    )
    reduce_out = lax.all_to_all(reduce_in, "tp", 0, 0, tiled=True).astype(jnp.float32)
    expert_part = expert_rows * col_share
    expert_sum = jnp.sum(
        reduce_out[:, :expert_part] + reduce_out[:, expert_part : 2 * expert_part], axis=0
    ).reshape(expert_rows, col_share)
    shared_sum = jnp.sum(reduce_out[:, 2 * expert_part :], axis=0).reshape(all_rows, 2 * unit_count)
    hidden_all = (jax.nn.silu(shared_sum[:, :unit_count]) * shared_sum[:, unit_count:]).astype(
        jnp.bfloat16
    )
    shared_down = jnp.dot(hidden_all, shared_w_down, preferred_element_type=jnp.float32)
    ey = expert_sum.astype(jnp.bfloat16).astype(jnp.float32)
    back_in = jnp.concatenate(
        [
            ey.reshape(req_count, capacity * col_share),
            shared_down.reshape(req_count, row_count * col_share),
        ],
        axis=1,
    )
    back = lax.all_to_all(back_in, "req", 0, 0, tiled=True)
    returned = back[:, : capacity * col_share].reshape(expert_count * capacity, col_share)
    shared_mine = jnp.sum(
        back[:, capacity * col_share :].reshape(req_count, row_count, col_share), axis=0
    )
    moe_out = jnp.dot(combine_map, returned, precision=HIGHEST)
    switch = jax.nn.sigmoid(jnp.dot(mixed, shared_switch, preferred_element_type=jnp.float32))
    resid_mine = lax.dynamic_slice_in_dim(resid, tp_index * col_share, col_share, 1)
    final = resid_mine + moe_out + switch[:, None] * shared_mine
    return final.astype(jnp.bfloat16).reshape(req_rows, step_count, col_share)


def solution(mesh):
    return jax.shard_map(
        per_device,
        mesh=mesh,
        in_specs=(
            P("req", None, None),
            P(),
            P(None, None, "tp"),
            P(None, "tp"),
            P("tp", None),
            P("req", None, "tp"),
            P("req", None, "tp"),
            P(),
            P(),
            P(),
            P("req", None, None),
            P("req", None, None),
            P("req", None, "tp"),
            P("req", None, "tp"),
            P("req", "tp", None),
            P("tp", "req"),
            P("tp", "req"),
            P("req", "tp"),
            P(),
        ),
        out_specs=P("req", None, "tp"),
        check_vma=False,
    )
```

profile of v0, /device:TPU:0, one launch (start us, length us, event | category | flops | bytes accessed | tf_op | source)
XLA Modules:
  0.0 155.8 jit_solution(10692810095028306036)
XLA Ops:
  0.0 0.9 dynamic_slice.9
  1.0 0.9 multiply_reduce_fusion.1
  1.9 0.7 convert_element_type.114
  2.6 0.7 convert_element_type.116
  3.3 3.8 %fusion.30 = f32[3,4,3,512]{3,1,2,0:T(4,128)S(1)} fusion(bf16[2048,3,512]{2,0,1:T(8,128)(2,1)} %param.21, bf16[3,4,2048]{2,1,0:T(4,128)(2,1)} %param.19, f32[2048]{0:T(1024)S(1)} %convert_element_type.114, f32[3,4]{1,0:T(4,128)S(1)} %add_rsqrt_fusion.1, f32[3,512]{1,0:T(4,128)S(1)} %convert_element_type.116), kind=kOutput, calls=%fused_computation.28 | convolution fusion | flops 75614208 | bytes 6428720 | tf_op jit(solution)/shard_map/rsd,dcf->rscf/dot_general | solution.py:81
  7.5 0.7 broadcast_in_dim.81
  8.1 7.3 %all-to-all-start = ((bf16[8,3,4,4,128]{4,3,2,1,0:T(4,128)(2,1)}), bf16[8,3,4,4,128]{4,3,2,1,0:T(4,128)(2,1)S(1)}, u32[]{:S(2)}, u32[]{:S(2)}) async-start(bf16[8,3,4,4,128]{4,3,2,1,0:T(4,128)(2,1)} %broadcast_in_dim.81), calls=%async_computation | async-start | bytes 196608 | tf_op jit(solution)/shard_map/all_to_all | solution.py:41
  15.9 0.8 gather_fusion
  17.2 5.3 %all-to-all-done = bf16[8,3,4,4,128]{4,3,2,1,0:T(4,128)(2,1)S(1)} async-done(((bf16[8,3,4,4,128]{4,3,2,1,0:T(4,128)(2,1)}), bf16[8,3,4,4,128]{4,3,2,1,0:T(4,128)(2,1)S(1)}, u32[]{:S(2)}, u32[]{:S(2)}) %all-to-all-start) | async-done | bytes 98336 | tf_op jit(solution)/shard_map/all_to_all | solution.py:41
  22.5 0.7 gather_fusion.1
  23.2 5.4 %fusion.134 = (f32[40,4,4]{1,2,0:T(4,128)S(1)}, f32[40,4,4,128]{3,1,2,0:T(4,128)S(1)}) fusion(bf16[40,4,4,128]{3,2,1,0:T(4,128)(2,1)S(1)} %gather_fusion.1, pred[40,128]{1,0:T(8,128)(4,1)S(1)} %fusion.97, bf16[40,128,512]{2,1,0:T(8,128)(2,1)} %param.24), kind=kOutput, calls=%fused_computation.184 | convolution fusion | flops 21216640 | bytes 5742080 | tf_op jit(solution)/shard_map/pshd,pkhd->pshk/dot_general | solution.py:104
  29.0 0.5 fusion.64
  29.5 4.0 %fusion.18 = f32[40,4,4,128]{3,1,2,0:T(4,128)S(1)} fusion(f32[40,4,4,128]{3,1,2,0:T(4,128)S(1)} %get-tuple-element.31, f32[40,4,4]{1,2,0:T(4,128)S(1)} %get-tuple-element.30, pred[40,128]{1,0:T(8,128)(4,1)S(1)} %fusion.97, bf16[40,128,512]{2,1,0:T(8,128)(2,1)} %param.25), kind=kOutput, calls=%fused_computation.22 | convolution fusion | flops 21217280 | bytes 5905920 | tf_op jit(solution)/shard_map/pshk,pkhd->pshd/dot_general | solution.py:112
  33.5 0.6 fusion.60
  34.2 0.5 fusion.67
  34.9 0.7 pad_maximum_fusion
  35.7 3.4 %all-to-all-start.1 = ((f32[24,17,128]{2,1,0:T(8,128)}), f32[24,17,128]{2,1,0:T(8,128)S(1)}, u32[]{:S(2)}, u32[]{:S(2)}) async-start(f32[24,17,128]{2,1,0:T(8,128)} %pad_maximum_fusion), calls=%async_computation.1 | async-start | bytes 589824 | tf_op jit(solution)/shard_map/all_to_all | solution.py:136
  39.4 8.3 %all-to-all-done.1 = f32[24,17,128]{2,1,0:T(8,128)S(1)} async-done(((f32[24,17,128]{2,1,0:T(8,128)}), f32[24,17,128]{2,1,0:T(8,128)S(1)}, u32[]{:S(2)}, u32[]{:S(2)}) %all-to-all-start.1) | async-done | bytes 208928 | tf_op jit(solution)/shard_map/all_to_all | solution.py:136
  48.8 0.4 fusion.140
  49.2 0.8 broadcast_in_dim.92
  50.0 3.5 %all-to-all-start.2 = ((f32[4,12,2048]{2,1,0:T(8,128)}), f32[4,12,2048]{2,1,0:T(8,128)S(1)}, u32[]{:S(2)}, u32[]{:S(2)}) async-start(f32[4,12,2048]{2,1,0:T(8,128)} %broadcast_in_dim.92), calls=%async_computation.2 | async-start | bytes 1048576 | tf_op jit(solution)/shard_map/all_to_all | solution.py:41
  53.6 0.3 convolution_convert_fusion.3
  53.8 8.5 %all-to-all-done.2 = f32[4,12,2048]{2,1,0:T(8,128)S(1)} async-done(((f32[4,12,2048]{2,1,0:T(8,128)}), f32[4,12,2048]{2,1,0:T(8,128)S(1)}, u32[]{:S(2)}, u32[]{:S(2)}) %all-to-all-start.2) | async-done | bytes 393248 | tf_op jit(solution)/shard_map/all_to_all | solution.py:41
  63.0 0.3 reshape.373
  63.3 0.5 broadcast.288
  63.9 0.8 reduce.3
  64.9 13.5 %all_to_all.48 = bf16[8,2,9216]{2,1,0:T(2,128)(2,1)S(1)} all-to-all(bf16[8,2,9216]{2,1,0:T(2,128)(2,1)S(1)} %reshape.410), channel_id=1, replica_groups=mesh['req'=8,'tp'=4] {'req'}, dimensions={0} | all-to-all | bytes 589824 | tf_op jit(solution)/shard_map/all_to_all | solution.py:211
  78.4 0.2 reshape.411
  78.8 0.2 reshape.374
  79.3 1.9 %fusion.13 = f32[48,352]{1,0:T(8,128)S(1)} fusion(bf16[48,2048]{1,0:T(8,128)(2,1)S(1)} %reshape.374, bf16[1,2048,352]{1,2,0:T(8,128)(2,1)} %param.31), kind=kOutput, calls=%fused_computation.19 | convolution fusion | flops 69206016 | bytes 1705984 | tf_op jit(solution)/shard_map/dot_general | solution.py:215
  81.2 2.9 %convert_bitcast_fusion = (bf16[1,4,48,512]{3,2,1,0:T(8,128)(2,1)S(1)}, bf16[1,4,48,512]{3,2,1,0:T(8,128)(2,1)S(1)}) fusion(bf16[44,4,8,512]{3,2,1,0:T(8,128)(2,1)} %bitcast.183, bf16[48,2048]{1,0:T(8,128)(2,1)S(1)} %reshape.374, bf16[1,2048,352]{1,2,0:T(8,128)(2,1)} %param.32, f32[48,352]{1,0:T(8,128)S(1)} %fusion.13), kind=kOutput, calls=%fused_computation.85 | convolution fusion | flops 138906624 | bytes 3540992 | tf_op jit(solution)/shard_map/dot_general | solution.py:218
  84.3 1.5 convolution_convert_fusion.1
  85.8 1.5 convolution_convert_fusion.2
  87.3 0.3 reshape.409
  87.9 5.0 %maximum_bitcast_fusion = bf16[4,1,184320]{2,0,1:T(4,128)(2,1)} fusion(bf16[4,24576]{1,0:T(4,128)(2,1)S(1)} %bitcast.191, bf16[4,24576]{1,0:T(4,128)(2,1)S(1)} %bitcast.190, bf16[184320]{0:T(1024)(128)(2,1)S(1)} %pad.4.clone), kind=kLoop, calls=%fused_computation.13 | loop fusion | flops 4423680 | bytes 2236416 | tf_op jit(solution)/shard_map/all_to_all | solution.py:239
  92.9 4.7 %reduce.4 = bf16[4,184320]{1,0:T(4,128)(2,1)} reduce(bf16[4,1,184320]{2,0,1:T(4,128)(2,1)} %maximum_bitcast_fusion, bf16[]{:T(256)} %broadcast.288), dimensions={1}, to_apply=%copy.166.reduce_sub_computation | reduce | bytes 2949122 | tf_op jit(solution)/shard_map/all_to_all | solution.py:239
  97.6 4.0 %reshape.412 = bf16[4,2,92160]{2,1,0:T(2,128)(2,1)} reshape(bf16[4,184320]{1,0:T(4,128)(2,1)} %reduce.4) | data formatting | bytes 2949120
  101.6 23.4 %all_to_all.49 = bf16[4,2,92160]{2,1,0:T(2,128)(2,1)} all-to-all(bf16[4,2,92160]{2,1,0:T(2,128)(2,1)} %reshape.412), channel_id=1, replica_groups=mesh['req'=8,'tp'=4] {'tp'}, dimensions={0} | all-to-all | bytes 2949120 | tf_op jit(solution)/shard_map/all_to_all | solution.py:239
  125.0 4.4 %reshape.413 = bf16[4,1,184320]{2,1,0:T(2,128)(2,1)} reshape(bf16[4,2,92160]{2,1,0:T(2,128)(2,1)} %all_to_all.49) | data formatting | bytes 2949120
  129.4 3.7 %copy.242 = f32[4,1,184320]{2,0,1:T(4,128)S(1)} copy(bf16[4,1,184320]{2,1,0:T(2,128)(2,1)} %reshape.413) | data formatting | bytes 4423680
  133.1 0.3 fusion.59
  133.4 5.6 %slice_reduce_fusion = f32[135168]{0:T(1024)S(1)} fusion(f32[4,184320]{1,0:T(4,128)S(1)} %bitcast.182), kind=kLoop, calls=%fused_computation.12 | loop fusion | flops 405504 | bytes 2703360 | tf_op jit(solution)/shard_map/reduce_sum | solution.py:244
  139.1 1.4 fusion.73
  140.6 0.9 all_to_all.39
  141.6 3.4 %all-to-all-start.5 = ((f32[8,1,9216]{2,1,0:T(1,128)}), f32[8,1,9216]{2,1,0:T(1,128)S(1)}, u32[]{:S(2)}, u32[]{:S(2)}) async-start(f32[8,1,9216]{2,1,0:T(1,128)} %all_to_all.39), calls=%async_computation.5 | async-start | bytes 589824 | tf_op jit(solution)/shard_map/all_to_all | solution.py:257
  145.1 0.3 fusion.94
  145.5 9.3 %all-to-all-done.5 = f32[8,1,9216]{2,1,0:T(1,128)S(1)} async-done(((f32[8,1,9216]{2,1,0:T(1,128)}), f32[8,1,9216]{2,1,0:T(1,128)S(1)}, u32[]{:S(2)}, u32[]{:S(2)}) %all-to-all-start.5) | async-done | bytes 294944 | tf_op jit(solution)/shard_map/all_to_all | solution.py:257
  155.2 0.6 reshape.381
  (99 shorter events, 5.9 us)
Async XLA Ops:
  0.0 48.8 %copy-start = (bf16[512,2048]{1,0:T(8,128)(2,1)S(1)}, bf16[512,2048]{1,0:T(8,128)(2,1)}, u32[]{:S(2)}) copy-start(bf16[512,2048]{1,0:T(8,128)(2,1)} %param.23) | copy-start | bytes 6291460
  3.3 12.1 %copy-start.4 = (s32[3,4,4]{2,1,0:T(4,128)S(1)}, s32[3,4,4]{2,1,0:T(4,128)}, u32[]{:S(2)}) copy-start(s32[3,4,4]{2,1,0:T(4,128)} %param.29) | copy-start | bytes 580
  3.3 12.2 %copy-start.3 = (s32[24,37]{1,0:T(8,128)S(1)}, s32[24,37]{1,0:T(8,128)}, u32[]{:S(2)}) copy-start(s32[24,37]{1,0:T(8,128)} %param.26) | copy-start | bytes 10660
  3.3 12.6 %copy-start.1 = (s32[24]{0:T(128)S(1)}, s32[24]{0:T(128)}, u32[]{:S(2)}) copy-start(s32[24]{0:T(128)} %param.27) | copy-start | bytes 292
  8.1 14.4 %all-to-all-start = ((bf16[8,3,4,4,128]{4,3,2,1,0:T(4,128)(2,1)}), bf16[8,3,4,4,128]{4,3,2,1,0:T(4,128)(2,1)S(1)}, u32[]{:S(2)}, u32[]{:S(2)}) async-start(bf16[8,3,4,4,128]{4,3,2,1,0:T(4,128)(2,1)} %broadcast_in_dim.81), calls=%async_computation | async-start | bytes 196608 | tf_op jit(solution)/shard_map/all_to_all | solution.py:41
  35.7 12.0 %all-to-all-start.1 = ((f32[24,17,128]{2,1,0:T(8,128)}), f32[24,17,128]{2,1,0:T(8,128)S(1)}, u32[]{:S(2)}, u32[]{:S(2)}) async-start(f32[24,17,128]{2,1,0:T(8,128)} %pad_maximum_fusion), calls=%async_computation.1 | async-start | bytes 589824 | tf_op jit(solution)/shard_map/all_to_all | solution.py:136
  39.1 14.4 %copy-start.2 = (bf16[3,4,2048]{2,1,0:T(4,128)(2,1)S(1)}, bf16[3,4,2048]{2,1,0:T(4,128)(2,1)}, u32[]{:S(2)}) copy-start(bf16[3,4,2048]{2,1,0:T(4,128)(2,1)} %param.19) | copy-start | bytes 147460
  39.3 14.2 %copy-start.6 = (bf16[2048]{0:T(1024)(128)(2,1)S(1)}, bf16[2048]{0:T(1024)(128)(2,1)}, u32[]{:S(2)}) copy-start(bf16[2048]{0:T(1024)(128)(2,1)} %param.28) | copy-start | bytes 12292
  50.0 12.3 %all-to-all-start.2 = ((f32[4,12,2048]{2,1,0:T(8,128)}), f32[4,12,2048]{2,1,0:T(8,128)S(1)}, u32[]{:S(2)}, u32[]{:S(2)}) async-start(f32[4,12,2048]{2,1,0:T(8,128)} %broadcast_in_dim.92), calls=%async_computation.2 | async-start | bytes 1048576 | tf_op jit(solution)/shard_map/all_to_all | solution.py:41
  138.9 6.1 %copy-start.5 = (f32[3,4,4]{2,1,0:T(4,128)S(1)}, f32[3,4,4]{2,1,0:T(4,128)}, u32[]{:S(2)}) copy-start(f32[3,4,4]{2,1,0:T(4,128)} %param.30) | copy-start | bytes 580
  138.9 6.1 %copy-start.7 = (bf16[2048]{0:T(1024)(128)(2,1)S(1)}, bf16[2048]{0:T(1024)(128)(2,1)}, u32[]{:S(2)}) copy-start(bf16[2048]{0:T(1024)(128)(2,1)} %param.37) | copy-start | bytes 12292
  141.6 13.3 %all-to-all-start.5 = ((f32[8,1,9216]{2,1,0:T(1,128)}), f32[8,1,9216]{2,1,0:T(1,128)S(1)}, u32[]{:S(2)}, u32[]{:S(2)}) async-start(f32[8,1,9216]{2,1,0:T(1,128)} %all_to_all.39), calls=%async_computation.5 | async-start | bytes 589824 | tf_op jit(solution)/shard_map/all_to_all | solution.py:257
where the time goes:
time: 157 us; the launch traced here: 156 us
  blocking collectives  36.9 us (24%)
  waiting for transfers between devices  31.4 us (20%)
  matrix products  25.4 us (16%)
  other arithmetic  22.2 us (14%)
  local copies, waits for them, and re-layouts  21.7 us (14%)
  starting transfers between devices  17.6 us (11%)
    all_to_all x1, blocking collectives, per_device(): lax.all_to_all(reduce_in, 'tp', 0, 0, tiled=True).astype(jnp.float32)  23.4 us
    all_to_all x2, waiting for transfers between devices, bcast_a2a(): lax.all_to_all(spread, axis, 0, 0, tiled=True)  13.8 us
    all_to_all x1, blocking collectives, per_device(): received = lax.all_to_all(dispatch, 'req', 0, 0, tiled=True)  13.5 us
    unnamed x29, local copies, waits for them, and re-layouts  13.2 us
    all_to_all x2, starting transfers between devices, bcast_a2a(): lax.all_to_all(spread, axis, 0, 0, tiled=True)  10.8 us
    all_to_all x2, other arithmetic, per_device(): lax.all_to_all(reduce_in, 'tp', 0, 0, tiled=True).astype(jnp.float32)  9.7 us
    all_to_all x1, waiting for transfers between devices, per_device(): back = lax.all_to_all(back_in, 'req', 0, 0, tiled=True)  9.34 us
    all_to_all x1, waiting for transfers between devices, per_device(): lax.all_to_all(packed, 'req', 0, 0, tiled=True)  8.27 us
  transfers between devices with their start and end apart: 4, of which 4 were waited for; matrix products, arithmetic and copies ran while one was open for 2% of the time, Pallas kernels for 0%

commit v1 on v0

--- a/solution.py
+++ b/solution.py
@@ -10,6 +10,28 @@
 EPS = 1e-06
 THETA = 1000000.0
 HIGHEST = lax.Precision.HIGHEST
+
+
+def in_blocks(x, dim, size):
+    before, after = (x.shape[:dim], x.shape[dim + 1 :])
+    return jnp.moveaxis(x.reshape(*before, size, -1, *after), dim, 0)
+
+
+def in_order(blocks, dim):
+    blocks = jnp.moveaxis(blocks, 0, dim)
+    shape = blocks.shape
+    return blocks.reshape(*shape[:dim], shape[dim] * shape[dim + 1], *shape[dim + 2 :])
+
+
+def swapped_with_each(value, axis, split_dim, concat_dim):
+    size, here = (lax.axis_size(axis), lax.axis_index(axis))
+    blocks = in_blocks(value, split_dim, size)
+    done = [blocks[here]]
+    for lap in range(1, size):
+        sent = blocks[here ^ lap]
+        done.append(lax.ppermute(sent, axis, [(i, i ^ lap) for i in range(size)]))
+    blocks = jnp.stack(done)[here ^ jnp.arange(size)]
+    return in_order(blocks, concat_dim)
 
 
 def rms_norm(inputs, gain_vector):
@@ -133,7 +155,7 @@
     packed = jnp.concatenate(
         [local_out.reshape(all_requests, stat_width, HD), stat_row[:, None, :]], axis=1
     )
-    gathered = lax.all_to_all(packed, "req", 0, 0, tiled=True).reshape(
+    gathered = swapped_with_each(packed, "req", 0, 0).reshape(
         req_count, req_rows, stat_width + 1, HD
     )
     part_out = gathered[:, :, :stat_width, :]

time: 157 us -> 161 us (1.025)
  starting transfers between devices: 17.6 us -> 23.9 us
    ppermute x0 -> x7, starting transfers between devices: none -> 9.68 us  [swapped_with_each(): done.append(lax.ppermute(sent, axis, [(i, i ^ lap) for i in range(size)]))]
    all_to_all x1 -> x0, waiting for transfers between devices: 8.27 us -> none  [per_device(): lax.all_to_all(packed, 'req', 0, 0, tiled=True)]
    ppermute x0 -> x7, waiting for transfers between devices: none -> 7.15 us  [swapped_with_each(): done.append(lax.ppermute(sent, axis, [(i, i ^ lap) for i in range(size)]))]
    all_to_all x1 -> x0, starting transfers between devices: 3.42 us -> none  [per_device(): lax.all_to_all(packed, 'req', 0, 0, tiled=True)]
    unnamed x29 -> x36, local copies, waits for them, and re-layouts: 13.2 us -> 13.3 us
  transfers between devices with their start and end apart: 4 -> 10, of which waited for: 4 -> 5; matrix products, arithmetic and copies ran while one was open for 2% -> 2% of each run, Pallas kernels for 0% -> 0%
where the time goes in v1:
time: 161 us; the launch traced here: 160 us
  blocking collectives  36.7 us (23%)
  waiting for transfers between devices  30 us (19%)
  matrix products  24.9 us (15%)
  starting transfers between devices  23.9 us (15%)
  local copies, waits for them, and re-layouts  22.5 us (14%)
  other arithmetic  21.6 us (13%)
    all_to_all x1, blocking collectives, per_device(): lax.all_to_all(reduce_in, 'tp', 0, 0, tiled=True).astype(jnp.float32)  23.4 us
    all_to_all x2, waiting for transfers between devices, bcast_a2a(): lax.all_to_all(spread, axis, 0, 0, tiled=True)  13.5 us
    all_to_all x1, blocking collectives, per_device(): received = lax.all_to_all(dispatch, 'req', 0, 0, tiled=True)  13.3 us
    unnamed x36, local copies, waits for them, and re-layouts  13.3 us
    all_to_all x2, starting transfers between devices, bcast_a2a(): lax.all_to_all(spread, axis, 0, 0, tiled=True)  10.7 us
    all_to_all x2, other arithmetic, per_device(): lax.all_to_all(reduce_in, 'tp', 0, 0, tiled=True).astype(jnp.float32)  9.7 us
    ppermute x7, starting transfers between devices, swapped_with_each(): done.append(lax.ppermute(sent, axis, [(i, i ^ lap) for i in range(size)]))  9.68 us
    all_to_all x1, waiting for transfers between devices, per_device(): back = lax.all_to_all(back_in, 'req', 0, 0, tiled=True)  9.34 us
  transfers between devices with their start and end apart: 10, of which 5 were waited for; matrix products, arithmetic and copies ran while one was open for 2% of the time, Pallas kernels for 0%

profile of v1, /device:TPU:0, one launch (start us, length us, event | category | flops | bytes accessed | tf_op | source)
XLA Modules:
  0.0 160.4 jit_solution(16037145637811731280)
XLA Ops:
  0.0 0.9 dynamic_slice.33
  1.0 0.9 multiply_reduce_fusion.2
  1.9 0.7 convert_element_type.114
  2.6 0.7 convert_element_type.116
  3.3 3.8 %fusion.30 = f32[3,4,3,512]{3,1,2,0:T(4,128)S(1)} fusion(bf16[2048,3,512]{2,0,1:T(8,128)(2,1)} %param.21, bf16[3,4,2048]{2,1,0:T(4,128)(2,1)} %param.19, f32[2048]{0:T(1024)S(1)} %convert_element_type.114, f32[3,4]{1,0:T(4,128)S(1)} %add_rsqrt_fusion.1, f32[3,512]{1,0:T(4,128)S(1)} %convert_element_type.116), kind=kOutput, calls=%fused_computation.30 | convolution fusion | flops 75614208 | bytes 6428720 | tf_op jit(solution)/shard_map/rsd,dcf->rscf/dot_general | solution.py:103
  7.5 0.7 broadcast_in_dim.79
  8.1 7.3 %all-to-all-start = ((bf16[8,3,4,4,128]{4,3,2,1,0:T(4,128)(2,1)}), bf16[8,3,4,4,128]{4,3,2,1,0:T(4,128)(2,1)S(1)}, u32[]{:S(2)}, u32[]{:S(2)}) async-start(bf16[8,3,4,4,128]{4,3,2,1,0:T(4,128)(2,1)} %broadcast_in_dim.79), calls=%async_computation | async-start | bytes 196608 | tf_op jit(solution)/shard_map/all_to_all | solution.py:63
  15.9 0.8 gather_fusion
  17.5 5.0 %all-to-all-done = bf16[8,3,4,4,128]{4,3,2,1,0:T(4,128)(2,1)S(1)} async-done(((bf16[8,3,4,4,128]{4,3,2,1,0:T(4,128)(2,1)}), bf16[8,3,4,4,128]{4,3,2,1,0:T(4,128)(2,1)S(1)}, u32[]{:S(2)}, u32[]{:S(2)}) %all-to-all-start) | async-done | bytes 98336 | tf_op jit(solution)/shard_map/all_to_all | solution.py:63
  22.5 0.7 gather_fusion.1
  23.2 5.4 %fusion.127 = (f32[40,4,4]{1,2,0:T(4,128)S(1)}, f32[40,4,4,128]{3,1,2,0:T(4,128)S(1)}) fusion(bf16[40,4,4,128]{3,2,1,0:T(4,128)(2,1)S(1)} %gather_fusion.1, pred[40,128]{1,0:T(8,128)(4,1)S(1)} %fusion.91, bf16[40,128,512]{2,1,0:T(8,128)(2,1)} %param.24), kind=kOutput, calls=%fused_computation.195 | convolution fusion | flops 21216640 | bytes 5742080 | tf_op jit(solution)/shard_map/pshd,pkhd->pshk/dot_general | solution.py:126
  29.1 0.5 fusion.62
  29.7 4.0 %fusion.18 = f32[40,4,4,128]{3,1,2,0:T(4,128)S(1)} fusion(f32[40,4,4,128]{3,1,2,0:T(4,128)S(1)} %get-tuple-element.39, f32[40,4,4]{1,2,0:T(4,128)S(1)} %get-tuple-element.38, pred[40,128]{1,0:T(8,128)(4,1)S(1)} %fusion.91, bf16[40,128,512]{2,1,0:T(8,128)(2,1)} %param.25), kind=kOutput, calls=%fused_computation.23 | convolution fusion | flops 21217280 | bytes 5905920 | tf_op jit(solution)/shard_map/pshk,pkhd->pshd/dot_general | solution.py:134
  33.7 0.6 convolution_bitcast_fusion
  35.0 0.4 collective-permute-start
  35.4 1.7 %collective-permute-start.6 = (f32[3,17,128]{2,1,0:T(8,128)S(1)}, f32[3,17,128]{2,1,0:T(8,128)S(1)}, u32[]{:S(2)}, u32[]{:S(2)}) collective-permute-start(f32[3,17,128]{2,1,0:T(8,128)S(1)} %get-tuple-element.20), channel_id=1, source_target_pairs={{0,28},{4,24},{8,20},{12,16},{16,12},{20,8},{24,4},{28,0},{1,29},{... | collective-permute-start | bytes 78344 | tf_op jit(solution)/shard_map/ppermute | solution.py:32
  37.1 3.3 %collective-permute-start.5 = (f32[3,17,128]{2,1,0:T(8,128)S(1)}, f32[3,17,128]{2,1,0:T(8,128)S(1)}, u32[]{:S(2)}, u32[]{:S(2)}) collective-permute-start(f32[3,17,128]{2,1,0:T(8,128)S(1)} %get-tuple-element.21), channel_id=1, source_target_pairs={{0,24},{4,28},{8,16},{12,20},{16,8},{20,12},{24,0},{28,4},{1,25},{... | collective-permute-start | bytes 78344 | tf_op jit(solution)/shard_map/ppermute | solution.py:32
  40.4 2.7 %collective-permute-start.3 = (f32[3,17,128]{2,1,0:T(8,128)S(1)}, f32[3,17,128]{2,1,0:T(8,128)S(1)}, u32[]{:S(2)}, u32[]{:S(2)}) collective-permute-start(f32[3,17,128]{2,1,0:T(8,128)S(1)} %get-tuple-element.23), channel_id=1, source_target_pairs={{0,16},{4,20},{8,24},{12,28},{16,0},{20,4},{24,8},{28,12},{1,17},{... | collective-permute-start | bytes 78344 | tf_op jit(solution)/shard_map/ppermute | solution.py:32
  43.1 3.9 %collective-permute-done.1 = f32[3,17,128]{2,1,0:T(8,128)S(1)} collective-permute-done((f32[3,17,128]{2,1,0:T(8,128)S(1)}, f32[3,17,128]{2,1,0:T(8,128)S(1)}, u32[]{:S(2)}, u32[]{:S(2)}) %collective-permute-start.1) | collective-permute-done | bytes 26144 | tf_op jit(solution)/shard_map/ppermute | solution.py:32
  47.0 1.7 %collective-permute-start.2 = (f32[3,17,128]{2,1,0:T(8,128)S(1)}, f32[3,17,128]{2,1,0:T(8,128)S(1)}, u32[]{:S(2)}, u32[]{:S(2)}) collective-permute-start(f32[3,17,128]{2,1,0:T(8,128)S(1)} %get-tuple-element.24), channel_id=1, source_target_pairs={{0,12},{4,8},{8,4},{12,0},{16,28},{20,24},{24,20},{28,16},{1,13},{... | collective-permute-start | bytes 78344 | tf_op jit(solution)/shard_map/ppermute | solution.py:32
  48.7 3.2 %collective-permute-done.2 = f32[3,17,128]{2,1,0:T(8,128)S(1)} collective-permute-done((f32[3,17,128]{2,1,0:T(8,128)S(1)}, f32[3,17,128]{2,1,0:T(8,128)S(1)}, u32[]{:S(2)}, u32[]{:S(2)}) %collective-permute-start.2) | collective-permute-done | bytes 26144 | tf_op jit(solution)/shard_map/ppermute | solution.py:32
  52.0 0.6 gather_fusion.2
  53.5 0.4 fusion.133
  53.9 0.8 broadcast_in_dim.89
  54.7 3.5 %all-to-all-start.1 = ((f32[4,12,2048]{2,1,0:T(8,128)}), f32[4,12,2048]{2,1,0:T(8,128)S(1)}, u32[]{:S(2)}, u32[]{:S(2)}) async-start(f32[4,12,2048]{2,1,0:T(8,128)} %broadcast_in_dim.89), calls=%async_computation.1 | async-start | bytes 1048576 | tf_op jit(solution)/shard_map/all_to_all | solution.py:63
  58.5 8.5 %all-to-all-done.1 = f32[4,12,2048]{2,1,0:T(8,128)S(1)} async-done(((f32[4,12,2048]{2,1,0:T(8,128)}), f32[4,12,2048]{2,1,0:T(8,128)S(1)}, u32[]{:S(2)}, u32[]{:S(2)}) %all-to-all-start.1) | async-done | bytes 393248 | tf_op jit(solution)/shard_map/all_to_all | solution.py:63
  68.0 0.5 broadcast.325
  68.5 0.8 reduce.5
  69.6 13.3 %all_to_all.43 = bf16[8,2,9216]{2,1,0:T(2,128)(2,1)S(1)} all-to-all(bf16[8,2,9216]{2,1,0:T(2,128)(2,1)S(1)} %reshape.432), channel_id=1, replica_groups=mesh['req'=8,'tp'=4] {'req'}, dimensions={0} | all-to-all | bytes 589824 | tf_op jit(solution)/shard_map/all_to_all | solution.py:233
  83.8 1.9 %fusion.13 = f32[48,352]{1,0:T(8,128)S(1)} fusion(bf16[48,2048]{1,0:T(8,128)(2,1)S(1)} %reshape.387, bf16[1,2048,352]{1,2,0:T(8,128)(2,1)} %param.31), kind=kOutput, calls=%fused_computation.20 | convolution fusion | flops 69206016 | bytes 1705984 | tf_op jit(solution)/shard_map/dot_general | solution.py:237
  85.7 2.9 %convert_bitcast_fusion = (bf16[1,4,48,512]{3,2,1,0:T(8,128)(2,1)S(1)}, bf16[1,4,48,512]{3,2,1,0:T(8,128)(2,1)S(1)}) fusion(bf16[44,4,8,512]{3,2,1,0:T(8,128)(2,1)} %bitcast.203, bf16[48,2048]{1,0:T(8,128)(2,1)S(1)} %reshape.387, bf16[1,2048,352]{1,2,0:T(8,128)(2,1)} %param.32, f32[48,352]{1,0:T(8,128)S(1)} %fusion.13), kind=kOutput, calls=%fused_computation.86 | convolution fusion | flops 138906624 | bytes 3540992 | tf_op jit(solution)/shard_map/dot_general | solution.py:240
  88.8 1.5 convolution_convert_fusion.1
  90.3 1.5 convolution_convert_fusion.2
  91.9 0.3 reshape.431
  92.4 5.0 %maximum_bitcast_fusion = bf16[4,1,184320]{2,0,1:T(4,128)(2,1)} fusion(bf16[4,24576]{1,0:T(4,128)(2,1)S(1)} %bitcast.209, bf16[4,24576]{1,0:T(4,128)(2,1)S(1)} %bitcast.208, bf16[184320]{0:T(1024)(128)(2,1)S(1)} %pad.4.clone), kind=kLoop, calls=%fused_computation.14 | loop fusion | flops 4423680 | bytes 2236416 | tf_op jit(solution)/shard_map/all_to_all | solution.py:261
  97.4 4.7 %reduce.6 = bf16[4,184320]{1,0:T(4,128)(2,1)} reduce(bf16[4,1,184320]{2,0,1:T(4,128)(2,1)} %maximum_bitcast_fusion, bf16[]{:T(256)} %broadcast.325), dimensions={1}, to_apply=%copy.226.reduce_sub_computation | reduce | bytes 2949122 | tf_op jit(solution)/shard_map/all_to_all | solution.py:261
  102.1 4.0 %reshape.434 = bf16[4,2,92160]{2,1,0:T(2,128)(2,1)} reshape(bf16[4,184320]{1,0:T(4,128)(2,1)} %reduce.6) | data formatting | bytes 2949120
  106.1 23.4 %all_to_all.44 = bf16[4,2,92160]{2,1,0:T(2,128)(2,1)} all-to-all(bf16[4,2,92160]{2,1,0:T(2,128)(2,1)} %reshape.434), channel_id=1, replica_groups=mesh['req'=8,'tp'=4] {'tp'}, dimensions={0} | all-to-all | bytes 2949120 | tf_op jit(solution)/shard_map/all_to_all | solution.py:261
  129.5 4.4 %reshape.435 = bf16[4,1,184320]{2,1,0:T(2,128)(2,1)} reshape(bf16[4,2,92160]{2,1,0:T(2,128)(2,1)} %all_to_all.44) | data formatting | bytes 2949120
  133.9 3.7 %copy.290 = f32[4,1,184320]{2,0,1:T(4,128)S(1)} copy(bf16[4,1,184320]{2,1,0:T(2,128)(2,1)} %reshape.435) | data formatting | bytes 4423680
  137.6 0.3 fusion.59
  137.9 5.6 %slice_reduce_fusion = f32[135168]{0:T(1024)S(1)} fusion(f32[4,184320]{1,0:T(4,128)S(1)} %bitcast.202), kind=kLoop, calls=%fused_computation.13 | loop fusion | flops 405504 | bytes 2703360 | tf_op jit(solution)/shard_map/reduce_sum | solution.py:266
  143.6 1.4 fusion.71
  145.2 0.9 all_to_all.35
  146.1 3.4 %all-to-all-start.4 = ((f32[8,1,9216]{2,1,0:T(1,128)}), f32[8,1,9216]{2,1,0:T(1,128)S(1)}, u32[]{:S(2)}, u32[]{:S(2)}) async-start(f32[8,1,9216]{2,1,0:T(1,128)} %all_to_all.35), calls=%async_computation.4 | async-start | bytes 589824 | tf_op jit(solution)/shard_map/all_to_all | solution.py:279
  149.6 0.3 fusion.88
  150.1 9.3 %all-to-all-done.4 = f32[8,1,9216]{2,1,0:T(1,128)S(1)} async-done(((f32[8,1,9216]{2,1,0:T(1,128)}), f32[8,1,9216]{2,1,0:T(1,128)S(1)}, u32[]{:S(2)}, u32[]{:S(2)}) %all-to-all-start.4) | async-done | bytes 294944 | tf_op jit(solution)/shard_map/all_to_all | solution.py:279
  159.8 0.6 reshape.394
  (122 shorter events, 7.3 us)
Async XLA Ops:
  0.0 53.5 %copy-start = (bf16[512,2048]{1,0:T(8,128)(2,1)S(1)}, bf16[512,2048]{1,0:T(8,128)(2,1)}, u32[]{:S(2)}) copy-start(bf16[512,2048]{1,0:T(8,128)(2,1)} %param.23) | copy-start | bytes 6291460
  3.3 12.2 %copy-start.4 = (s32[3,4,4]{2,1,0:T(4,128)S(1)}, s32[3,4,4]{2,1,0:T(4,128)}, u32[]{:S(2)}) copy-start(s32[3,4,4]{2,1,0:T(4,128)} %param.29) | copy-start | bytes 580
  3.3 12.3 %copy-start.3 = (s32[24,37]{1,0:T(8,128)S(1)}, s32[24,37]{1,0:T(8,128)}, u32[]{:S(2)}) copy-start(s32[24,37]{1,0:T(8,128)} %param.26) | copy-start | bytes 10660
  3.3 12.6 %copy-start.1 = (s32[24]{0:T(128)S(1)}, s32[24]{0:T(128)}, u32[]{:S(2)}) copy-start(s32[24]{0:T(128)} %param.27) | copy-start | bytes 292
  8.1 14.4 %all-to-all-start = ((bf16[8,3,4,4,128]{4,3,2,1,0:T(4,128)(2,1)}), bf16[8,3,4,4,128]{4,3,2,1,0:T(4,128)(2,1)S(1)}, u32[]{:S(2)}, u32[]{:S(2)}) async-start(bf16[8,3,4,4,128]{4,3,2,1,0:T(4,128)(2,1)} %broadcast_in_dim.79), calls=%async_computation | async-start | bytes 196608 | tf_op jit(solution)/shard_map/all_to_all | solution.py:63
  35.0 8.0 %collective-permute-start = (f32[3,17,128]{2,1,0:T(8,128)S(1)}, f32[3,17,128]{2,1,0:T(8,128)S(1)}, u32[]{:S(2)}, u32[]{:S(2)}) collective-permute-start(f32[3,17,128]{2,1,0:T(8,128)S(1)} %get-tuple-element.26), channel_id=1, source_target_pairs={{0,4},{4,0},{8,12},{12,8},{16,20},{20,16},{24,28},{28,24},{1,5},{5... | collective-permute-start | bytes 78344 | tf_op jit(solution)/shard_map/ppermute | solution.py:32
  35.4 16.5 %collective-permute-start.6 = (f32[3,17,128]{2,1,0:T(8,128)S(1)}, f32[3,17,128]{2,1,0:T(8,128)S(1)}, u32[]{:S(2)}, u32[]{:S(2)}) collective-permute-start(f32[3,17,128]{2,1,0:T(8,128)S(1)} %get-tuple-element.20), channel_id=1, source_target_pairs={{0,28},{4,24},{8,20},{12,16},{16,12},{20,8},{24,4},{28,0},{1,29},{... | collective-permute-start | bytes 78344 | tf_op jit(solution)/shard_map/ppermute | solution.py:32
  37.1 14.8 %collective-permute-start.5 = (f32[3,17,128]{2,1,0:T(8,128)S(1)}, f32[3,17,128]{2,1,0:T(8,128)S(1)}, u32[]{:S(2)}, u32[]{:S(2)}) collective-permute-start(f32[3,17,128]{2,1,0:T(8,128)S(1)} %get-tuple-element.21), channel_id=1, source_target_pairs={{0,24},{4,28},{8,16},{12,20},{16,8},{20,12},{24,0},{28,4},{1,25},{... | collective-permute-start | bytes 78344 | tf_op jit(solution)/shard_map/ppermute | solution.py:32
  40.4 11.5 %collective-permute-start.4 = (f32[3,17,128]{2,1,0:T(8,128)S(1)}, f32[3,17,128]{2,1,0:T(8,128)S(1)}, u32[]{:S(2)}, u32[]{:S(2)}) collective-permute-start(f32[3,17,128]{2,1,0:T(8,128)S(1)} %get-tuple-element.22), channel_id=1, source_target_pairs={{0,20},{4,16},{8,28},{12,24},{16,4},{20,0},{24,12},{28,8},{1,21},{... | collective-permute-start | bytes 78344 | tf_op jit(solution)/shard_map/ppermute | solution.py:32
  40.4 11.5 %collective-permute-start.3 = (f32[3,17,128]{2,1,0:T(8,128)S(1)}, f32[3,17,128]{2,1,0:T(8,128)S(1)}, u32[]{:S(2)}, u32[]{:S(2)}) collective-permute-start(f32[3,17,128]{2,1,0:T(8,128)S(1)} %get-tuple-element.23), channel_id=1, source_target_pairs={{0,16},{4,20},{8,24},{12,28},{16,0},{20,4},{24,8},{28,12},{1,17},{... | collective-permute-start | bytes 78344 | tf_op jit(solution)/shard_map/ppermute | solution.py:32
  43.1 4.0 %collective-permute-start.1 = (f32[3,17,128]{2,1,0:T(8,128)S(1)}, f32[3,17,128]{2,1,0:T(8,128)S(1)}, u32[]{:S(2)}, u32[]{:S(2)}) collective-permute-start(f32[3,17,128]{2,1,0:T(8,128)S(1)} %get-tuple-element.25), channel_id=1, source_target_pairs={{0,8},{4,12},{8,0},{12,4},{16,24},{20,28},{24,16},{28,20},{1,9},{5... | collective-permute-start | bytes 78344 | tf_op jit(solution)/shard_map/ppermute | solution.py:32
  47.0 4.9 %collective-permute-start.2 = (f32[3,17,128]{2,1,0:T(8,128)S(1)}, f32[3,17,128]{2,1,0:T(8,128)S(1)}, u32[]{:S(2)}, u32[]{:S(2)}) collective-permute-start(f32[3,17,128]{2,1,0:T(8,128)S(1)} %get-tuple-element.24), channel_id=1, source_target_pairs={{0,12},{4,8},{8,4},{12,0},{16,28},{20,24},{24,20},{28,16},{1,13},{... | collective-permute-start | bytes 78344 | tf_op jit(solution)/shard_map/ppermute | solution.py:32
  51.9 6.3 %copy-start.2 = (bf16[3,4,2048]{2,1,0:T(4,128)(2,1)S(1)}, bf16[3,4,2048]{2,1,0:T(4,128)(2,1)}, u32[]{:S(2)}) copy-start(bf16[3,4,2048]{2,1,0:T(4,128)(2,1)} %param.19) | copy-start | bytes 147460
  52.0 6.3 %copy-start.6 = (bf16[2048]{0:T(1024)(128)(2,1)S(1)}, bf16[2048]{0:T(1024)(128)(2,1)}, u32[]{:S(2)}) copy-start(bf16[2048]{0:T(1024)(128)(2,1)} %param.28) | copy-start | bytes 12292
  54.7 12.3 %all-to-all-start.1 = ((f32[4,12,2048]{2,1,0:T(8,128)}), f32[4,12,2048]{2,1,0:T(8,128)S(1)}, u32[]{:S(2)}, u32[]{:S(2)}) async-start(f32[4,12,2048]{2,1,0:T(8,128)} %broadcast_in_dim.89), calls=%async_computation.1 | async-start | bytes 1048576 | tf_op jit(solution)/shard_map/all_to_all | solution.py:63
  143.5 6.1 %copy-start.5 = (f32[3,4,4]{2,1,0:T(4,128)S(1)}, f32[3,4,4]{2,1,0:T(4,128)}, u32[]{:S(2)}) copy-start(f32[3,4,4]{2,1,0:T(4,128)} %param.30) | copy-start | bytes 580
  143.5 6.1 %copy-start.7 = (bf16[2048]{0:T(1024)(128)(2,1)S(1)}, bf16[2048]{0:T(1024)(128)(2,1)}, u32[]{:S(2)}) copy-start(bf16[2048]{0:T(1024)(128)(2,1)} %param.37) | copy-start | bytes 12292
  146.1 13.3 %all-to-all-start.4 = ((f32[8,1,9216]{2,1,0:T(1,128)}), f32[8,1,9216]{2,1,0:T(1,128)S(1)}, u32[]{:S(2)}, u32[]{:S(2)}) async-start(f32[8,1,9216]{2,1,0:T(1,128)} %all_to_all.35), calls=%async_computation.4 | async-start | bytes 589824 | tf_op jit(solution)/shard_map/all_to_all | solution.py:279
